TPU v7x, 512 devices: a whole 4x4x16 slice. The times are simulated.
512 devices in a mesh: seq: 64 (over x, z), tp: 8 (over y, core).
Axes of the slice: x: 4, y: 4, z: 16, core: 2. Of those that a mesh axis runs over, the one named last changes fastest.
Arguments:
- queries: bfloat16 [64, 4, 8192], P('seq', None, 'tp'), may hold values from -40 to 40
- new_keys: bfloat16 [64, 4, 1024], P('seq', None, 'tp'), may hold values from -6 to 6
- new_values: bfloat16 [64, 4, 1024], P('seq', None, 'tp'), may hold values from -6 to 6
- prefix_keys: bfloat16 [8, 12288, 1024], P(None, 'seq', 'tp'), may hold values from -8 to 8
- prefix_values: bfloat16 [8, 12288, 1024], P(None, 'seq', 'tp'), may hold values from -6 to 6
- page_keys: bfloat16 [1024, 64, 1024], P('seq', None, 'tp'), may hold values from -6 to 6
- page_values: bfloat16 [1024, 64, 1024], P('seq', None, 'tp'), may hold values from -6 to 6
- out_weight: bfloat16 [8192, 8192], P('tp', 'seq'), may hold values from -0.5 to 0.5
- group_of: int32 [64], replicated, may hold values from 0 to 7, as said below
- prefix_len: int32 [8], replicated, may hold values from 2 to 12288, as said below
- total_len: int32 [64], replicated, may hold values from 3 to 16384, as said below
- page_owner: int32 [1024], P('seq'), may hold values from 0 to 63, as said below
- page_slot: int32 [1024], P('seq'), may hold values from 0 to 63, as said below
- new_valid: int32 [64, 4], replicated, may hold values from 0 to 1, as said below
Outputs:
- attn_out: bfloat16 [256, 8192], P('tp', 'seq')
Inputs may be any that keep to these rules, and one draw needn't show every extreme that they name: `group_of`: every one of the 8 groups has at least one request. `prefix_len`: some group's prefix holds exactly 12288 tokens. `page_owner`: every request owns at least one page and at most 64 pages; one request owns exactly 64. `page_slot`: the pages of one request carry the slots 0, 1, 2 and so on, each once. A request's pages are full except the one of its highest slot, which holds 1 to 64 tokens; total_len is its group's prefix length plus these tokens. `new_valid`: each row is a run of ones followed by zeros, and its first entry is one.
All inputs are finite; a program needn't handle non-finite values.
Results may differ from a plain program's by a relative error of at most 0.022.
Values may be sent and summed in bfloat16 or wider, within the bound.
No kernel may reach another device: no remote copies, remote signals or barrier semaphores. Data moves between devices by JAX's collectives and lax.ppermute only.
A program may use at most 192 MiB of HBM per device.

v0:
```python
import jax
import jax.numpy as jnp
from jax import lax
from jax.sharding import PartitionSpec as P

HEAD_DIM = 128
HPK = 8
GROUPS = 8
NEW = 4
NEG = -1e30


def local(
    queries,
    new_keys,
    new_values,
    prefix_keys,
    prefix_values,
    page_keys,
    page_values,
    out_weight,
    group_of,
    prefix_len,
    total_len,
    page_owner,
    page_slot,
    new_valid,
):
    req_dev = queries.shape[0]
    seq_count = lax.axis_size("seq")
    requests = req_dev * seq_count
    kv_local = new_keys.shape[2] // HEAD_DIM
    heads_local = kv_local * HPK
    score_scale = HEAD_DIM ** (-0.5)
    seq_idx = lax.axis_index("seq")
    gathered = lax.all_gather(queries, "seq", axis=0, tiled=True)
    query_all = gathered.reshape(requests, NEW, kv_local, HPK, HEAD_DIM)
    group_hot = group_of[:, None] == jnp.arange(GROUPS, dtype=jnp.int32)[None, :]
    own_prefix = jnp.sum(jnp.where(group_hot, prefix_len[None, :], 0), axis=1)
    suffix_len = total_len - own_prefix
    pre_dev = prefix_keys.shape[1]
    page_count = page_keys.shape[0]
    page_len = page_keys.shape[1]
    keys = jnp.concatenate(
        [
            prefix_keys.reshape(GROUPS * pre_dev, kv_local, HEAD_DIM),
            page_keys.reshape(page_count * page_len, kv_local, HEAD_DIM),
            new_keys.reshape(req_dev * NEW, kv_local, HEAD_DIM),
        ],
        axis=0,
    )
    values = jnp.concatenate(
        [
            prefix_values.reshape(GROUPS * pre_dev, kv_local, HEAD_DIM),
            page_values.reshape(page_count * page_len, kv_local, HEAD_DIM),
            new_values.reshape(req_dev * NEW, kv_local, HEAD_DIM),
        ],
        axis=0,
    )
    req_ids = jnp.arange(requests, dtype=jnp.int32)
    positions = seq_idx * pre_dev + jnp.arange(pre_dev, dtype=jnp.int32)
    pre_live = positions[None, :] < prefix_len[:, None]
    pre_mask = group_hot[:, :, None] & pre_live[None, :, :]
    pre_mask = pre_mask.reshape(requests, 1, GROUPS * pre_dev)
    pre_mask = jnp.broadcast_to(pre_mask, (requests, NEW, GROUPS * pre_dev))
    owner_hot = req_ids[:, None] == page_owner[None, :]
    offsets = page_slot[:, None] * page_len + jnp.arange(page_len, dtype=jnp.int32)[None, :]
    page_live = offsets[None, :, :] < suffix_len[:, None, None]
    page_mask = (owner_hot[:, :, None] & page_live).reshape(requests, 1, page_count * page_len)
    page_mask = jnp.broadcast_to(page_mask, (requests, NEW, page_count * page_len))
    new_owner = seq_idx * req_dev + jnp.arange(req_dev, dtype=jnp.int32)
    tok = jnp.arange(NEW, dtype=jnp.int32)
    causal = tok[None, :] <= tok[:, None]
    new_live = new_valid == 1
    new_mask = (
        (req_ids[:, None, None, None] == new_owner[None, None, :, None])
        & causal[None, :, None, :]
        & new_live[:, None, None, :]
    ).reshape(requests, NEW, req_dev * NEW)
    key_mask = jnp.concatenate([pre_mask, page_mask, new_mask], axis=2)
    key_mask = key_mask[:, :, None, None, :]
    scores = (
        jnp.einsum("rjkhd,nkd->rjkhn", query_all, keys, preferred_element_type=jnp.float32)
        * score_scale
    )
    masked = jnp.where(key_mask, scores, NEG)
    row_peak = jnp.max(masked, axis=-1)
    weights = jnp.where(key_mask, jnp.exp(masked - row_peak[..., None]), 0.0)
    row_total = jnp.sum(weights, axis=-1)
    out = jnp.einsum(
        "rjkhn,nkd->rjkhd", weights.astype(jnp.bfloat16), values, preferred_element_type=jnp.float32
    )
    top_peak = lax.pmax(row_peak, "seq")
    factor = jnp.exp(row_peak - top_peak)
    final_total, final_out = lax.psum((row_total * factor, out * factor[..., None]), "seq")
    valid_rows = new_valid.astype(jnp.float32)[:, :, None, None, None]
    attention = (final_out / final_total[..., None] * valid_rows).astype(jnp.bfloat16)
    attention = attention.reshape(requests * NEW, heads_local * HEAD_DIM)
    terms = jnp.dot(attention, out_weight, preferred_element_type=jnp.float32)
    summed = lax.psum_scatter(terms.astype(jnp.bfloat16), "tp", scatter_dimension=0, tiled=True)
    return summed


def solution(mesh):
    placed = (
        P("seq", None, "tp"),
        P("seq", None, "tp"),
        P("seq", None, "tp"),
        P(None, "seq", "tp"),
        P(None, "seq", "tp"),
        P("seq", None, "tp"),
        P("seq", None, "tp"),
        P("tp", "seq"),
        P(),
        P(),
        P(),
        P("seq"),
        P("seq"),
        P(),
    )
    return jax.shard_map(
        local, mesh=mesh, in_specs=placed, out_specs=P("tp", "seq"), check_vma=False
    )
```

profile of v0, /device:TPU:4, one launch (start us, length us, event | category | flops | bytes accessed | tf_op | source)
XLA Modules:
  0.0 738.8 jit_solution(732492033588366109)
XLA Ops:
  6.5 0.0 copy-start
  6.5 0.0 all-reduce.2.cloned.1.call-start
  6.5 0.8 broadcast_reduce_fusion.1
  7.3 0.7 iota_compare_fusion.1
  8.1 0.8 select_reduce_fusion
  9.0 0.1 lt.39
  9.0 0.1 lt.41
  9.1 0.1 and.61
  9.3 0.3 and.62
  9.5 0.7 broadcast_compare_fusion
  10.2 0.1 copy.20
  10.3 0.7 iota_compare_fusion
  11.0 0.2 and.65
  11.2 0.2 and.66
  11.4 0.7 broadcast_multiply_fusion
  12.1 0.1 broadcast_reduce_fusion
  12.2 0.1 add.40
  12.2 0.1 add.42
  12.3 106.2 %all_gather.3 = bf16[64,4,1024]{2,1,0:T(4,128)(2,1)S(1)} all-gather(bf16[1,4,1024]{2,1,0:T(4,128)(2,1)} %param.14), channel_id=1, replica_groups=mesh['seq'=64,'tp'=8] {'seq'}, dimensions={0}, use_global_device_ids=true | all-gather | bytes 532480 | tf_op jit(solution)/shard_map/all_gather | solution.py:36
  118.6 0.2 reshape.221
  118.8 0.1 broadcast_and_fusion
  118.9 0.7 sub.14
  119.5 0.1 and_and_fusion
  119.6 0.1 compare_and_fusion
  119.7 0.1 broadcast_in_dim.30
  119.8 0.1 broadcast_in_dim.33
  119.9 0.1 pad_add_fusion
  120.0 0.0 copy-start.3
  120.0 0.0 copy-start.4
  120.0 0.0 copy-start.5
  120.0 5.5 fusion
  125.5 0.0 copy-start.1
  125.5 7.3 copy-done.1
  132.8 7.2 fusion.1
  140.0 236.7 %pmax.7 = f32[64,4,1,8]{0,3,1,2:T(8,128)S(1)} all-reduce(f32[64,4,1,8]{0,3,1,2:T(8,128)S(1)} %bitcast.79), channel_id=1, replica_groups=mesh['seq'=64,'tp'=8] {'seq'}, use_global_device_ids=true, to_apply=%region_2.3 | all-reduce | flops 2048 | bytes 16384 | tf_op jit(solution)/shard_map/pmax | solution.py:93
  376.8 0.0 copy-done.3
  376.8 0.0 copy-done.4
  376.8 0.0 copy-start.2
  376.8 10.4 %fusion.13 = f32[64,4,1,8,128]{4,0,3,1,2:T(8,128)} fusion(f32[2564,64,4,8]{0,1,3,2:T(8,128)} %copy-done.1, f32[64,4,8]{0,2,1:T(8,128)S(1)} %get-tuple-element.7, pred[64,4,2564]{2,0,1:T(8,128)(4,1)S(1)} %pad_add_fusion, bf16[4,1,128]{2,0,1:T(4,128)(2,1)S(1)} %bitcast.85, bf16[1024,1,128]{2,0,1:T(8,128)(2,1)S(1)} %bitcast.83, ...), kind=kOutput, calls=%fused_computation.11 | convolution fusion | flops 1372761088 | bytes 23382016 | tf_op jit(solution)/shard_map/rjkhn,nkd->rjkhd/dot_general | solution.py:90
  387.2 0.0 all-reduce.2.cloned.1.call-update
  387.2 0.0 reduce-scatter.2.cloned.1.call-start
  387.3 266.2 %psum.15 = f32[64,4,8]{0,2,1:T(8,128)S(1)} all-reduce(f32[64,4,8]{0,2,1:T(8,128)S(1)} %get-tuple-element.5), channel_id=1, replica_groups=mesh['seq'=64,'tp'=8] {'seq'}, use_global_device_ids=true, to_apply=%region_5.6 | all-reduce | flops 2048 | bytes 16384 | tf_op jit(solution)/shard_map/psum | solution.py:95
  653.5 37.7 %all-reduce.2.cloned.1.call-done = f32[64,4,1,8,128]{4,0,3,1,2:T(8,128)} async-done(((f32[64,4,1,8,128]{4,0,3,1,2:T(8,128)}), f32[64,4,1,8,128]{4,0,3,1,2:T(8,128)}) %all-reduce.2.cloned.1.call-update) | async-done | bytes 1048592 | tf_op jit(solution)/shard_map/psum | solution.py:95
  691.2 1.6 multiply_convert_fusion
  692.8 0.3 copy.23
  693.2 0.9 convolution_convert_fusion
  694.1 0.0 reduce-scatter.2.cloned.1.call-update
  694.1 37.9 %reduce-scatter.2.cloned.1.call-done = bf16[32,128]{1,0:T(8,128)(2,1)} async-done(((bf16[256,128]{1,0:T(8,128)(2,1)}), bf16[32,128]{1,0:T(8,128)(2,1)}) %reduce-scatter.2.cloned.1.call-update) | async-done | bytes 8208 | tf_op jit(solution)/shard_map/reduce_scatter | solution.py:100
  (12 shorter events, 0.1 us)
Async XLA Ops:
  6.5 686.6 %copy-start = (bf16[1024,128]{1,0:T(8,128)(2,1)S(1)}, bf16[1024,128]{1,0:T(8,128)(2,1)}, u32[]{:S(2)}) copy-start(bf16[1024,128]{1,0:T(8,128)(2,1)} %param.21) | copy-start | bytes 786436
  6.5 684.6 %all-reduce.2.cloned.1.call-start = ((), (), s32[]{:S(2)}) async-start(), calls=%async_computation.1 | async-start | bytes 2097152 | tf_op jit(solution)/shard_map/psum | solution.py:95
  120.0 256.8 %copy-start.3 = (bf16[8,192,128]{2,1,0:T(8,128)(2,1)S(1)}, bf16[8,192,128]{2,1,0:T(8,128)(2,1)}, u32[]{:S(2)}) copy-start(bf16[8,192,128]{2,1,0:T(8,128)(2,1)} %param.18) | copy-start | bytes 1179652
  120.0 256.8 %copy-start.4 = (bf16[16,64,128]{2,1,0:T(8,128)(2,1)S(1)}, bf16[16,64,128]{2,1,0:T(8,128)(2,1)}, u32[]{:S(2)}) copy-start(bf16[16,64,128]{2,1,0:T(8,128)(2,1)} %param.20) | copy-start | bytes 786436
  120.0 256.8 %copy-start.5 = (bf16[1,4,128]{2,1,0:T(4,128)(2,1)S(1)}, bf16[1,4,128]{2,1,0:T(4,128)(2,1)}, u32[]{:S(2)}) copy-start(bf16[1,4,128]{2,1,0:T(4,128)(2,1)} %param.16) | copy-start | bytes 3076
  125.5 7.3 copy-start.1
  376.8 10.5 %copy-start.2 = (s32[64,4]{0,1:T(4,128)S(1)}, s32[64,4]{0,1:T(4,128)}, u32[]{:S(2)}) copy-start(s32[64,4]{0,1:T(4,128)} %param.27) | copy-start | bytes 3076
  387.2 344.8 %reduce-scatter.2.cloned.1.call-start = ((), (), s32[]{:S(2)}) async-start(), calls=%async_computation.2 | async-start | bytes 73728 | tf_op jit(solution)/shard_map/reduce_scatter | solution.py:100
Sparse Core Ops, SparseCore 0:
  387.3 303.7 all-reduce.1
  694.2 37.7 reduce-scatter.1
where the time goes:
time: 739 us
  blocking collectives  609 us (82%)
  waiting for transfers between devices  75.6 us (10%)
  matrix products  16.7 us (2%)
  between operations  13.7 us (2%)
  other arithmetic  13.4 us (2%)
  local copies, waits for them, and re-layouts  10.2 us (1%)
    psum x1, blocking collectives, local(): lax.psum((row_total * factor, out * factor[..., None]), 'seq')  266 us
    pmax x1, blocking collectives, local(): top_peak = lax.pmax(row_peak, 'seq')  237 us
    all_gather x1, blocking collectives, local(): gathered = lax.all_gather(queries, 'seq', axis=0, tiled=True)  106 us
    reduce_scatter x1, waiting for transfers between devices, local(): lax.psum_scatter(terms.astype(jnp.bfloat16), 'tp', scatter_dimension=0, t...  37.9 us
    psum x1, waiting for transfers between devices, local(): lax.psum((row_total * factor, out * factor[..., None]), 'seq')  37.7 us
  transfers between devices with their start and end apart: 2, of which 2 were waited for; matrix products, arithmetic and copies ran while one was open for 0% of the time, Pallas kernels for 0%

commit v1 on v0

--- a/solution.py
+++ b/solution.py
@@ -33,7 +33,9 @@
     heads_local = kv_local * HPK
     score_scale = HEAD_DIM ** (-0.5)
     seq_idx = lax.axis_index("seq")
-    gathered = lax.all_gather(queries, "seq", axis=0, tiled=True)
+    gathered = jnp.concatenate(
+        lax.all_to_all(jnp.stack([queries] * lax.axis_size("seq")), "seq", 0, 0), axis=0
+    )
     query_all = gathered.reshape(requests, NEW, kv_local, HPK, HEAD_DIM)
     group_hot = group_of[:, None] == jnp.arange(GROUPS, dtype=jnp.int32)[None, :]
     own_prefix = jnp.sum(jnp.where(group_hot, prefix_len[None, :], 0), axis=1)

time: 739 us -> 676 us (0.915)
  the two profiles are of different devices: /device:TPU:4 before, /device:TPU:2 now
where the time goes in v1:
time: 676 us
  blocking collectives  525 us (78%)
  waiting for transfers between devices  76 us (11%)
  starting transfers between devices  18.7 us (3%)
  matrix products  16.7 us (2%)
  between operations  13.7 us (2%)
  other arithmetic  13.4 us (2%)
  local copies, waits for them, and re-layouts  11.8 us (2%)
    psum x1, blocking collectives, local(): lax.psum((row_total * factor, out * factor[..., None]), 'seq')  274 us
    pmax x1, blocking collectives, local(): top_peak = lax.pmax(row_peak, 'seq')  251 us
    reduce_scatter x1, waiting for transfers between devices, local(): lax.psum_scatter(terms.astype(jnp.bfloat16), 'tp', scatter_dimension=0, t...  37.5 us
    all_to_all x1, waiting for transfers between devices, local(): lax.all_to_all(jnp.stack([queries] * lax.axis_size('seq')), 'seq', 0, 0)  24.7 us
    all_to_all x1, starting transfers between devices, local(): lax.all_to_all(jnp.stack([queries] * lax.axis_size('seq')), 'seq', 0, 0)  18.6 us
    psum x1, waiting for transfers between devices, local(): lax.psum((row_total * factor, out * factor[..., None]), 'seq')  13.8 us
  transfers between devices with their start and end apart: 3, of which 3 were waited for; matrix products, arithmetic and copies ran while one was open for 1% of the time, Pallas kernels for 0%

profile of v1, /device:TPU:2, one launch (start us, length us, event | category | flops | bytes accessed | tf_op | source)
XLA Modules:
  0.0 675.7 jit_solution(12783928072095828557)
XLA Ops:
  6.5 0.0 copy-start
  6.5 1.7 stack.2
  8.2 18.6 %all-to-all-start = ((bf16[64,1,4,1024]{3,2,1,0:T(4,128)(2,1)}), bf16[64,1,4,1024]{3,2,1,0:T(4,128)(2,1)S(1)}, u32[]{:S(2)}, u32[]{:S(2)}) async-start(bf16[64,1,4,1024]{3,2,1,0:T(4,128)(2,1)} %stack.2), calls=%async_computation | async-start | bytes 1048576 | tf_op jit(solution)/shard_map/all_to_all | solution.py:37
  26.9 0.0 all-reduce.2.cloned.1.call-start
  26.9 0.1 lt.39
  27.0 0.7 broadcast_reduce_fusion.1
  27.8 0.1 lt.41
  27.8 0.7 iota_compare_fusion.1
  28.6 0.1 and.61
  28.7 0.3 and.62
  29.0 0.7 broadcast_compare_fusion
  29.7 0.1 copy.19
  29.8 0.7 iota_compare_fusion
  30.4 0.2 and.65
  30.6 0.2 and.66
  30.9 0.7 broadcast_multiply_fusion
  31.5 0.1 broadcast_reduce_fusion
  31.6 0.1 add.40
  31.7 0.1 add.42
  31.8 0.8 select_reduce_fusion
  32.6 0.7 sub.14
  33.3 0.1 and_and_fusion
  33.4 0.1 compare_and_fusion
  33.5 0.1 broadcast_and_fusion
  33.6 0.1 broadcast_in_dim.30
  33.7 0.1 broadcast_in_dim.33
  33.8 0.1 pad_add_fusion
  33.9 24.7 %all-to-all-done = bf16[64,1,4,1024]{3,2,1,0:T(4,128)(2,1)S(1)} async-done(((bf16[64,1,4,1024]{3,2,1,0:T(4,128)(2,1)}), bf16[64,1,4,1024]{3,2,1,0:T(4,128)(2,1)S(1)}, u32[]{:S(2)}, u32[]{:S(2)}) %all-to-all-start) | async-done | bytes 524320 | tf_op jit(solution)/shard_map/all_to_all | solution.py:37
  58.5 0.2 reshape.223
  58.7 0.0 copy-start.3
  58.7 0.0 copy-start.4
  58.8 0.0 copy-start.5
  58.8 5.5 fusion
  64.3 7.3 %copy-done.1 = f32[2564,64,4,8]{0,1,3,2:T(8,128)} copy-done((f32[2564,64,4,8]{0,1,3,2:T(8,128)}, f32[2564,64,4,8]{0,1,3,2:T(8,128)S(1)}, u32[]{:S(2)}) %copy-start.1) | copy-done | bytes 21004312
  71.6 7.2 %fusion.1 = f32[64,4,8]{0,2,1:T(8,128)S(1)} fusion(f32[2564,64,4,8]{0,1,3,2:T(8,128)S(1)} %get-tuple-element.8, f32[64,4,8]{0,2,1:T(8,128)S(1)} %get-tuple-element.7, pred[64,4,2564]{2,0,1:T(8,128)(4,1)S(1)} %pad_add_fusion), kind=kLoop, calls=%fused_computation.3 | loop fusion | flops 26253312 | bytes 21677056 | tf_op jit(solution)/shard_map/reduce_sum | solution.py:91
  78.8 251.1 %pmax.7 = f32[64,4,1,8]{0,3,1,2:T(8,128)S(1)} all-reduce(f32[64,4,1,8]{0,3,1,2:T(8,128)S(1)} %bitcast.80), channel_id=1, replica_groups=mesh['seq'=64,'tp'=8] {'seq'}, use_global_device_ids=true, to_apply=%region_2.3 | all-reduce | flops 2048 | bytes 16384 | tf_op jit(solution)/shard_map/pmax | solution.py:95
  329.9 0.0 copy-done.3
  330.0 0.0 copy-start.2
  330.0 10.4 %fusion.13 = f32[64,4,1,8,128]{4,0,3,1,2:T(8,128)} fusion(f32[2564,64,4,8]{0,1,3,2:T(8,128)} %copy-done.1, f32[64,4,8]{0,2,1:T(8,128)S(1)} %get-tuple-element.7, pred[64,4,2564]{2,0,1:T(8,128)(4,1)S(1)} %pad_add_fusion, bf16[4,1,128]{2,0,1:T(4,128)(2,1)S(1)} %bitcast.87, bf16[1024,1,128]{2,0,1:T(8,128)(2,1)S(1)} %bitcast.85, ...), kind=kOutput, calls=%fused_computation.11 | convolution fusion | flops 1372761088 | bytes 23382016 | tf_op jit(solution)/shard_map/rjkhn,nkd->rjkhd/dot_general | solution.py:92
  340.3 0.0 all-reduce.2.cloned.1.call-update
  340.4 0.0 reduce-scatter.2.cloned.1.call-start
  340.4 274.2 %psum.15 = f32[64,4,8]{0,2,1:T(8,128)S(1)} all-reduce(f32[64,4,8]{0,2,1:T(8,128)S(1)} %get-tuple-element.5), channel_id=1, replica_groups=mesh['seq'=64,'tp'=8] {'seq'}, use_global_device_ids=true, to_apply=%region_5.6 | all-reduce | flops 2048 | bytes 16384 | tf_op jit(solution)/shard_map/psum | solution.py:97
  614.6 13.8 %all-reduce.2.cloned.1.call-done = f32[64,4,1,8,128]{4,0,3,1,2:T(8,128)} async-done(((f32[64,4,1,8,128]{4,0,3,1,2:T(8,128)}), f32[64,4,1,8,128]{4,0,3,1,2:T(8,128)}) %all-reduce.2.cloned.1.call-update) | async-done | bytes 1048592 | tf_op jit(solution)/shard_map/psum | solution.py:97
  628.4 1.6 multiply_convert_fusion
  630.1 0.3 copy.22
  630.4 0.9 convolution_convert_fusion
  631.3 0.0 reduce-scatter.2.cloned.1.call-update
  631.4 37.5 %reduce-scatter.2.cloned.1.call-done = bf16[32,128]{1,0:T(8,128)(2,1)} async-done(((bf16[256,128]{1,0:T(8,128)(2,1)}), bf16[32,128]{1,0:T(8,128)(2,1)}) %reduce-scatter.2.cloned.1.call-update) | async-done | bytes 8208 | tf_op jit(solution)/shard_map/reduce_scatter | solution.py:102
  (14 shorter events, 0.1 us)
Async XLA Ops:
  6.5 623.9 %copy-start = (bf16[1024,128]{1,0:T(8,128)(2,1)S(1)}, bf16[1024,128]{1,0:T(8,128)(2,1)}, u32[]{:S(2)}) copy-start(bf16[1024,128]{1,0:T(8,128)(2,1)} %param.21) | copy-start | bytes 786436
  8.2 50.3 %all-to-all-start = ((bf16[64,1,4,1024]{3,2,1,0:T(4,128)(2,1)}), bf16[64,1,4,1024]{3,2,1,0:T(4,128)(2,1)S(1)}, u32[]{:S(2)}, u32[]{:S(2)}) async-start(bf16[64,1,4,1024]{3,2,1,0:T(4,128)(2,1)} %stack.2), calls=%async_computation | async-start | bytes 1048576 | tf_op jit(solution)/shard_map/all_to_all | solution.py:37
  26.9 601.6 %all-reduce.2.cloned.1.call-start = ((), (), s32[]{:S(2)}) async-start(), calls=%async_computation.2 | async-start | bytes 2097152 | tf_op jit(solution)/shard_map/psum | solution.py:97
  58.7 271.2 %copy-start.3 = (bf16[8,192,128]{2,1,0:T(8,128)(2,1)S(1)}, bf16[8,192,128]{2,1,0:T(8,128)(2,1)}, u32[]{:S(2)}) copy-start(bf16[8,192,128]{2,1,0:T(8,128)(2,1)} %param.18) | copy-start | bytes 1179652
  58.7 271.2 %copy-start.4 = (bf16[16,64,128]{2,1,0:T(8,128)(2,1)S(1)}, bf16[16,64,128]{2,1,0:T(8,128)(2,1)}, u32[]{:S(2)}) copy-start(bf16[16,64,128]{2,1,0:T(8,128)(2,1)} %param.20) | copy-start | bytes 786436
  58.8 271.2 %copy-start.5 = (bf16[1,4,128]{2,1,0:T(4,128)(2,1)S(1)}, bf16[1,4,128]{2,1,0:T(4,128)(2,1)}, u32[]{:S(2)}) copy-start(bf16[1,4,128]{2,1,0:T(4,128)(2,1)} %param.16) | copy-start | bytes 3076
  64.2 7.3 %copy-start.1 = (f32[2564,64,4,8]{0,1,3,2:T(8,128)}, f32[2564,64,4,8]{0,1,3,2:T(8,128)S(1)}, u32[]{:S(2)}) copy-start(f32[2564,64,4,8]{0,1,3,2:T(8,128)S(1)} %get-tuple-element.8) | copy-start | bytes 63012868
  330.0 10.5 %copy-start.2 = (s32[64,4]{0,1:T(4,128)S(1)}, s32[64,4]{0,1:T(4,128)}, u32[]{:S(2)}) copy-start(s32[64,4]{0,1:T(4,128)} %param.27) | copy-start | bytes 3076
  340.4 328.5 %reduce-scatter.2.cloned.1.call-start = ((), (), s32[]{:S(2)}) async-start(), calls=%async_computation.3 | async-start | bytes 73728 | tf_op jit(solution)/shard_map/reduce_scatter | solution.py:102
Sparse Core Ops, SparseCore 0:
  340.5 287.9 all-reduce.1
  631.5 37.3 reduce-scatter.1
